TPU v7x, 32 devices: a whole 2x2x4 slice. The times are simulated.
32 devices in a mesh: groups: 2 (over y), pairs: 4 (over z), mp: 4 (over x, core).
Axes of the slice: x: 2, y: 2, z: 4, core: 2. Of those that a mesh axis runs over, the one named last changes fastest.
Arguments:
- tokens: bfloat16 [512, 768], P(('groups', 'pairs'), 'mp'), parts along dimension 0, may hold values from -6 to 6
- pair_list: int32 [16, 2], P(('groups', 'pairs')), parts along dimension 0, may hold values from 0 to 7, as said below
- confidence: float32 [16, 64], P(('groups', 'pairs')), parts along dimension 0, may hold values from 0.1 to 10
- gain_self: float32 [768], replicated, may hold values from 0.1 to 1.9
- gain_query: float32 [768], replicated, may hold values from 0.1 to 1.9
- gain_context: float32 [768], replicated, may hold values from 0.1 to 1.9
- gain_mlp: float32 [768], replicated, may hold values from 0.1 to 1.9
- self_qkv: bfloat16 [3, 768, 768], P(None, None, 'mp'), may hold values from -1 to 1
- self_out: bfloat16 [768, 768], P('mp'), may hold values from -0.21875 to 0.21875
- cross_query: bfloat16 [768, 768], P(None, 'mp'), may hold values from -1 to 1
- cross_kv: bfloat16 [2, 768, 768], P(None, None, 'mp'), may hold values from -1 to 1
- cross_out: bfloat16 [768, 768], P('mp'), may hold values from -0.21875 to 0.21875
- mlp_up: bfloat16 [768, 3072], P(None, 'mp'), may hold values from -0.21875 to 0.21875
- mlp_down: bfloat16 [3072, 768], P('mp'), may hold values from -0.109375 to 0.109375
Outputs:
- image_features: bfloat16 [512, 768], P(('groups', 'pairs'), 'mp'), parts along dimension 0
There are 2 independent parts, one for each index of `groups`. A program takes and returns all parts, laid end to end along the dimension named above; an argument that names none is the same for every part. Nothing has to cross between parts.
Inputs may be any that keep to these rules, and one draw needn't show every extreme that they name: `pair_list`: in each block of 2 consecutive pairs the 4 images named are distinct and have distinct owners, the owner of image i being i // 2; the images of each owner are named in exactly 4 blocks; some images are named by no pair.
All inputs are finite; a program needn't handle non-finite values.
Results may differ from a plain program's by a relative error of at most 0.012.
Values may be sent and summed in bfloat16 or wider, within the bound.
No kernel may reach another device: no remote copies, remote signals or barrier semaphores. Data moves between devices by JAX's collectives and lax.ppermute only.
A program may use at most 64 MiB of HBM per device.

v0:
```python
import jax
import jax.numpy as jnp
from jax import lax
from jax.sharding import PartitionSpec as P

HEAD = 64
TOKS = 32
EPSILON = 1e-06


def layer_norm(values, gain):
    center = values - jnp.mean(values, axis=-1, keepdims=True)
    spread = jnp.mean(center * center, axis=-1, keepdims=True)
    return (center * lax.rsqrt(spread + EPSILON) * gain).astype(jnp.bfloat16)


def attend(query, keys, values, views_n):
    rows_n, width = query.shape
    heads_n = width // HEAD
    qh = query.reshape(views_n, TOKS, heads_n, HEAD)
    kh = keys.reshape(views_n, TOKS, heads_n, HEAD)
    vh = values.reshape(views_n, TOKS, heads_n, HEAD)
    scores = jnp.einsum("vqhc,vkhc->vhqk", qh, kh, preferred_element_type=jnp.float32) * HEAD ** (
        -0.5
    )
    probs = jax.nn.softmax(scores, axis=-1).astype(jnp.bfloat16)
    mixed = jnp.einsum("vhqk,vkhc->vqhc", probs, vh, preferred_element_type=jnp.float32)
    return mixed.astype(jnp.bfloat16).reshape(rows_n, width)


def partner(values):
    shape = values.shape
    paired = values.reshape((shape[0] // 2, 2) + shape[1:])
    return jnp.flip(paired, axis=1).reshape(shape)


def summed_full(term):
    return lax.psum(term.astype(jnp.bfloat16), "mp").astype(jnp.float32)


def per_device(
    tokens,
    pair_list,
    confidence,
    gain_self,
    gain_query,
    gain_context,
    gain_mlp,
    self_qkv,
    self_out,
    cross_query,
    cross_kv,
    cross_out,
    mlp_up,
    mlp_down,
):
    quarter = tokens.shape[1]
    img_dev = tokens.shape[0] // TOKS
    pair_dev = pair_list.shape[0]
    views_n = 2 * pair_dev
    owners_n = lax.axis_size("pairs")
    own = lax.axis_index("pairs")
    table = lax.all_gather(pair_list, "pairs", axis=0, tiled=True).reshape(owners_n, views_n)
    wanted = jnp.where(table // img_dev == own, table % img_dev, -1)
    chosen = jnp.max(wanted, axis=1)
    images = tokens.reshape(img_dev, TOKS, quarter)
    picked = jnp.take(images, jnp.maximum(chosen, 0), axis=0)
    outgoing = jnp.where((chosen >= 0)[:, None, None], picked, jnp.zeros_like(picked))
    arrived = lax.all_to_all(outgoing, "pairs", split_axis=0, concat_axis=0, tiled=True)
    source = pair_list.reshape(views_n) // img_dev
    slices = jnp.take(arrived, source, axis=0)
    start = lax.all_gather(slices, "mp", axis=2, tiled=True)
    width = start.shape[2]
    rows_n = views_n * TOKS
    begin = start.astype(jnp.float32).reshape(rows_n, width)
    context = layer_norm(partner(start.astype(jnp.float32)), gain_context).reshape(rows_n, width)
    offset = lax.axis_index("mp") * quarter
    normed = layer_norm(begin, gain_self)
    qkv = jnp.einsum("rd,kdc->krc", normed, self_qkv, preferred_element_type=jnp.float32).astype(
        jnp.bfloat16
    )
    term = jnp.dot(
        attend(qkv[0], qkv[1], qkv[2], views_n), self_out, preferred_element_type=jnp.float32
    )
    resid = begin + summed_full(term)
    normed = layer_norm(resid, gain_query)
    query = jnp.dot(normed, cross_query, preferred_element_type=jnp.float32).astype(jnp.bfloat16)
    keyval = jnp.einsum(
        "rd,kdc->krc", context, cross_kv, preferred_element_type=jnp.float32
    ).astype(jnp.bfloat16)
    term = jnp.dot(
        attend(query, keyval[0], keyval[1], views_n), cross_out, preferred_element_type=jnp.float32
    )
    resid = resid + summed_full(term)
    normed = layer_norm(resid, gain_mlp)
    hidden = jax.nn.gelu(
        jnp.dot(normed, mlp_up, preferred_element_type=jnp.float32), approximate=False
    )
    term = jnp.dot(hidden.astype(jnp.bfloat16), mlp_down, preferred_element_type=jnp.float32)
    resid = resid + summed_full(term)
    final = lax.dynamic_slice_in_dim(resid, offset, quarter, 1)
    conf = confidence.reshape(views_n, TOKS)
    weighted = (final.reshape(views_n, TOKS, quarter) * conf[:, :, None]).reshape(
        views_n, TOKS * quarter
    )
    route = (source[None, :] == jnp.arange(owners_n)[:, None]).astype(jnp.float32)
    back = jnp.dot(route, weighted, precision=lax.Precision.HIGHEST).astype(jnp.bfloat16)
    back_weight = jnp.dot(route, conf, precision=lax.Precision.HIGHEST).astype(jnp.bfloat16)
    got_feat, got_weight = (
        lax.all_to_all(
            back.reshape(owners_n, TOKS, quarter), "pairs", split_axis=0, concat_axis=0, tiled=True
        ),
        lax.all_to_all(back_weight, "pairs", split_axis=0, concat_axis=0, tiled=True),
    )
    owner_match = chosen[None, :] == jnp.arange(img_dev)[:, None]
    numer = jnp.einsum(
        "ij,jtc->itc",
        owner_match.astype(jnp.bfloat16),
        got_feat,
        preferred_element_type=jnp.float32,
    )
    denom = jnp.dot(
        owner_match.astype(jnp.float32),
        got_weight.astype(jnp.float32),
        precision=lax.Precision.HIGHEST,
    )
    result = numer / jnp.maximum(denom, 1.0)[:, :, None]
    return result.astype(jnp.bfloat16).reshape(img_dev * TOKS, quarter)


def solution(mesh):
    return jax.shard_map(
        per_device,
        mesh=mesh,
        in_specs=(
            P(("groups", "pairs"), "mp"),
            P(("groups", "pairs"), None),
            P(("groups", "pairs"), None),
            P(),
            P(),
            P(),
            P(),
            P(None, None, "mp"),
            P("mp", None),
            P(None, "mp"),
            P(None, None, "mp"),
            P("mp", None),
            P(None, "mp"),
            P("mp", None),
        ),
        out_specs=P(("groups", "pairs"), "mp"),
        check_vma=False,
    )
```

profile of v0, /device:TPU:0, one launch (start us, length us, event | category | flops | bytes accessed | tf_op | source)
XLA Modules:
  0.0 180.7 jit_solution(869110114710449456)
XLA Ops:
  6.5 13.0 %all-gather = s32[4,2,2]{2,1,0:T(2,128)S(1)} all-gather(s32[1,2,2]{2,1,0:T(2,128)} %bitcast.90), channel_id=1, replica_groups=mesh['groups'=2,'pairs'=4,'mp'=4] {'pairs'}, dimensions={0}, use_global_device_ids=true | all-gather | bytes 80 | tf_op jit(solution)/shard_map/all_gather | solution.py:63
  19.7 0.1 reduce_max.36
  19.9 0.5 copy-done.11
  20.4 1.3 gather_fusion
  21.7 0.7 select_select_fusion
  22.4 3.3 %all-to-all-start = ((bf16[4,32,192]{2,1,0:T(8,128)(2,1)}), bf16[4,32,192]{2,1,0:T(8,128)(2,1)S(1)}, u32[]{:S(2)}, u32[]{:S(2)}) async-start(bf16[4,32,192]{2,1,0:T(8,128)(2,1)} %select_select_fusion), calls=%async_computation | async-start | bytes 131072 | tf_op jit(solution)/shard_map/all_to_all | solution.py:69
  25.7 0.8 reshape.277
  26.5 0.8 reshape.275
  27.3 0.5 compare_and_fusion
  27.8 3.6 %all-to-all-done = bf16[4,32,192]{2,1,0:T(8,128)(2,1)S(1)} async-done(((bf16[4,32,192]{2,1,0:T(8,128)(2,1)}), bf16[4,32,192]{2,1,0:T(8,128)(2,1)S(1)}, u32[]{:S(2)}, u32[]{:S(2)}) %all-to-all-start) | async-done | bytes 49184 | tf_op jit(solution)/shard_map/all_to_all | solution.py:69
  31.4 0.5 gather_fusion.1
  32.0 0.2 copy.73
  32.2 8.6 %all_gather.7 = bf16[4,32,768]{1,0,2:T(4,128)(2,1)S(1)} all-gather(bf16[4,32,192]{1,0,2:T(4,128)(2,1)S(1)} %copy.73), channel_id=1, replica_groups=mesh['groups'=2,'pairs'=4,'mp'=4] {'mp'}, dimensions={2}, use_global_device_ids=true | all-gather | bytes 245760 | tf_op jit(solution)/shard_map/all_gather | solution.py:72
  40.8 0.8 convert_reduce_fusion
  41.6 0.4 copy.74
  42.1 0.8 multiply_reduce_fusion.1
  42.9 0.7 div.88
  43.6 1.3 convert_element_type.84
  44.9 7.5 %rev.4 = f32[2,2,32,768]{2,1,0,3:T(2,128)S(1)} reverse(f32[2,2,32,768]{2,1,0,3:T(2,128)} %bitcast.83), dimensions={1} | reverse | bytes 786432 | tf_op jit(solution)/shard_map/jit(_flip)/rev | solution.py:34
  52.4 0.8 reduce_sum.93
  53.2 1.1 multiply_reduce_fusion
  54.4 0.6 copy.83
  55.2 0.8 fusion.18
  56.0 1.6 fusion.122
  57.6 0.1 reshape.312
  57.7 0.1 reshape.313
  57.9 0.2 convolution_multiply_fusion.1
  58.2 0.1 reshape.311
  58.4 0.3 fusion.6
  58.6 0.1 copy.82
  58.7 0.1 reshape.279
  58.9 0.9 convolution_convert_fusion.3
  59.9 0.1 fusion.15
  60.1 0.3 fusion.123
  60.5 0.1 reshape.316
  60.6 0.1 reshape.314
  60.7 28.6 %all-reduce.4.cloned.1.call-done = bf16[128,768]{1,0:T(8,128)(2,1)} async-done(((bf16[128,768]{1,0:T(8,128)(2,1)}), bf16[128,768]{1,0:T(8,128)(2,1)}) %all-reduce.4.cloned.1.call-update) | async-done | bytes 196624 | tf_op jit(solution)/shard_map/psum | solution.py:38
  89.3 1.0 fusion.77
  90.4 1.1 multiply_reduce_fusion.3
  91.5 0.3 convolution_convert_fusion.6
  91.8 0.1 reshape.315
  92.0 0.2 convolution_multiply_fusion
  92.3 0.3 fusion.7
  92.7 0.1 reshape.283
  92.8 0.9 convolution_convert_fusion.2
  93.9 31.7 %all-reduce.6.cloned.1.call-done = bf16[128,768]{1,0:T(8,128)(2,1)} async-done(((bf16[128,768]{1,0:T(8,128)(2,1)}), bf16[128,768]{1,0:T(8,128)(2,1)}) %all-reduce.6.cloned.1.call-update) | async-done | bytes 196624 | tf_op jit(solution)/shard_map/psum | solution.py:38
  125.6 1.1 fusion.117
  126.7 0.2 multiply_reduce_fusion.2
  126.9 2.1 %convolution_convert_fusion.1 = bf16[128,768]{1,0:T(8,128)(2,1)} fusion(bf16[768,768]{1,0:T(8,128)(2,1)S(1)} %copy-done, bf16[768,768]{1,0:T(8,128)(2,1)S(1)} %copy-done.13, f32[128,768]{1,0:T(8,128)S(1)} %get-tuple-element.6, f32[768]{0:T(1024)S(1)} %copy-done.14, f32[128]{0:T(128)S(1)} %add_rsqrt_fusion.2, f32[128]{0:T(128)S(1)} %broadcast_multiply_fusion.2), kind=kOutput, calls=%fused_computation.9 | convolution fusion | flops 308871168 | bytes 2953216 | tf_op jit(solution)/shard_map/dot_general | solution.py:99
  129.1 0.1 fusion.9
  129.2 0.6 copy.94
  129.8 4.6 %all-to-all-start.2 = ((bf16[4,1,32]{2,1,0:T(2,128)(2,1)}), bf16[4,1,32]{2,1,0:T(2,128)(2,1)S(1)}, u32[]{:S(2)}, u32[]{:S(2)}) async-start(bf16[4,1,32]{2,1,0:T(2,128)(2,1)} %copy.94), calls=%async_computation.2 | async-start | bytes 4096 | tf_op jit(solution)/shard_map/all_to_all | solution.py:113
  134.5 0.1 mul.147
  134.6 26.3 %all-reduce.8.cloned.1.call-done = bf16[128,768]{1,0:T(8,128)(2,1)} async-done(((bf16[128,768]{1,0:T(8,128)(2,1)}), bf16[128,768]{1,0:T(8,128)(2,1)}) %all-reduce.8.cloned.1.call-update) | async-done | bytes 196624 | tf_op jit(solution)/shard_map/psum | solution.py:38
  160.9 1.0 dynamic-slice_add_fusion
  161.9 0.1 reshape.284
  162.1 0.2 convolution_convert_fusion
  162.3 0.7 reshape.285
  163.0 4.6 %all-to-all-start.1 = ((bf16[4,32,192]{2,1,0:T(8,128)(2,1)}), bf16[4,32,192]{2,1,0:T(8,128)(2,1)S(1)}, u32[]{:S(2)}, u32[]{:S(2)}) async-start(bf16[4,32,192]{2,1,0:T(8,128)(2,1)} %reshape.285), calls=%async_computation.1 | async-start | bytes 131072 | tf_op jit(solution)/shard_map/all_to_all | solution.py:110
  167.6 0.1 convolution_maximum_fusion
  167.7 0.1 copy.95
  167.8 5.5 %all-to-all-done.1 = bf16[4,32,192]{2,1,0:T(8,128)(2,1)S(1)} async-done(((bf16[4,32,192]{2,1,0:T(8,128)(2,1)}), bf16[4,32,192]{2,1,0:T(8,128)(2,1)S(1)}, u32[]{:S(2)}, u32[]{:S(2)}) %all-to-all-start.1) | async-done | bytes 49184 | tf_op jit(solution)/shard_map/all_to_all | solution.py:110
  173.4 0.2 fusion.8
  173.5 0.6 copy.96
  (65 shorter events, 1.3 us)
Async XLA Ops:
  6.5 120.3 %copy-start = (bf16[768,768]{1,0:T(8,128)(2,1)S(1)}, bf16[768,768]{1,0:T(8,128)(2,1)}, u32[]{:S(2)}) copy-start(bf16[768,768]{1,0:T(8,128)(2,1)} %param.27) | copy-start | bytes 3538948
  19.8 0.5 copy-start.11
  22.4 9.0 %all-to-all-start = ((bf16[4,32,192]{2,1,0:T(8,128)(2,1)}), bf16[4,32,192]{2,1,0:T(8,128)(2,1)S(1)}, u32[]{:S(2)}, u32[]{:S(2)}) async-start(bf16[4,32,192]{2,1,0:T(8,128)(2,1)} %select_select_fusion), calls=%async_computation | async-start | bytes 131072 | tf_op jit(solution)/shard_map/all_to_all | solution.py:69
  25.7 63.6 %all-reduce.4.cloned.1.call-start = ((), (), s32[]{:S(2)}) async-start(), calls=%async_computation.3 | async-start | bytes 393216 | tf_op jit(solution)/shard_map/psum | solution.py:38
  53.2 1.9 %copy-start.6 = (f32[768]{0:T(1024)S(1)}, f32[768]{0:T(1024)}, u32[]{:S(2)}) copy-start(f32[768]{0:T(1024)} %param.17) | copy-start | bytes 9220
  57.6 1.3 copy-start.3
  57.9 2.0 %copy-start.7 = (f32[768]{0:T(1024)S(1)}, f32[768]{0:T(1024)}, u32[]{:S(2)}) copy-start(f32[768]{0:T(1024)} %param.19) | copy-start | bytes 9220
  58.2 1.9 %copy-start.2 = (bf16[2,768,192]{1,2,0:T(8,128)(2,1)S(1)}, bf16[2,768,192]{1,2,0:T(8,128)(2,1)}, u32[]{:S(2)}) copy-start(bf16[2,768,192]{1,2,0:T(8,128)(2,1)} %param.24) | copy-start | bytes 1769476
  59.8 65.8 %all-reduce.6.cloned.1.call-start = ((), (), s32[]{:S(2)}) async-start(), calls=%async_computation.4 | async-start | bytes 393216 | tf_op jit(solution)/shard_map/psum | solution.py:38
  60.1 31.4 %copy-start.4 = (bf16[768,192]{0,1:T(8,128)(2,1)S(1)}, bf16[768,192]{0,1:T(8,128)(2,1)}, u32[]{:S(2)}) copy-start(bf16[768,192]{0,1:T(8,128)(2,1)} %param.23) | copy-start | bytes 884740
  60.1 31.4 %copy-start.8 = (f32[768]{0:T(1024)S(1)}, f32[768]{0:T(1024)}, u32[]{:S(2)}) copy-start(f32[768]{0:T(1024)} %param.18) | copy-start | bytes 9220
  91.5 1.3 copy-start.5
  92.0 1.8 copy-start.9
  92.0 33.6 %copy-start.1 = (bf16[128,768]{1,0:T(8,128)(2,1)S(1)}, bf16[128,768]{1,0:T(8,128)(2,1)}, u32[]{:S(2)}) copy-start(bf16[128,768]{1,0:T(8,128)(2,1)} %all-reduce.4.cloned.1.call-done) | copy-start | bytes 589828
  92.6 34.3 %copy-start.14 = (f32[768]{0:T(1024)S(1)}, f32[768]{0:T(1024)}, u32[]{:S(2)}) copy-start(f32[768]{0:T(1024)} %param.20) | copy-start | bytes 9220
  93.7 67.2 %all-reduce.8.cloned.1.call-start = ((), (), s32[]{:S(2)}) async-start(), calls=%async_computation.5 | async-start | bytes 393216 | tf_op jit(solution)/shard_map/psum | solution.py:38
  93.9 33.0 %copy-start.13 = (bf16[768,768]{1,0:T(8,128)(2,1)S(1)}, bf16[768,768]{1,0:T(8,128)(2,1)}, u32[]{:S(2)}) copy-start(bf16[768,768]{1,0:T(8,128)(2,1)} %param.26) | copy-start | bytes 3538948
  126.9 2.2 %copy-start.10 = (s32[4]{0:T(128)S(1)}, s32[4]{0:T(128)}, u32[]{:S(2)}) copy-start(s32[4]{0:T(128)} %get-tuple-element.8) | copy-start | bytes 52
  129.1 38.6 %copy-start.12 = (s32[4]{0:T(128)S(1)}, s32[4]{0:T(128)}, u32[]{:S(2)}) copy-start(s32[4]{0:T(128)} %copy-done.11) | copy-start | bytes 52
  129.8 33.2 %all-to-all-start.2 = ((bf16[4,1,32]{2,1,0:T(2,128)(2,1)}), bf16[4,1,32]{2,1,0:T(2,128)(2,1)S(1)}, u32[]{:S(2)}, u32[]{:S(2)}) async-start(bf16[4,1,32]{2,1,0:T(2,128)(2,1)} %copy.94), calls=%async_computation.2 | async-start | bytes 4096 | tf_op jit(solution)/shard_map/all_to_all | solution.py:113
  163.0 10.3 %all-to-all-start.1 = ((bf16[4,32,192]{2,1,0:T(8,128)(2,1)}), bf16[4,32,192]{2,1,0:T(8,128)(2,1)S(1)}, u32[]{:S(2)}, u32[]{:S(2)}) async-start(bf16[4,32,192]{2,1,0:T(8,128)(2,1)} %reshape.285), calls=%async_computation.1 | async-start | bytes 131072 | tf_op jit(solution)/shard_map/all_to_all | solution.py:110
Sparse Core Ops, SparseCore 0:
  59.9 29.3 all-reduce.3
  93.8 31.7 all-reduce.5
  129.2 31.6 all-reduce.7
where the time goes:
time: 181 us
  waiting for transfers between devices  95.8 us (53%)
  blocking collectives  21.6 us (12%)
  local copies, waits for them, and re-layouts  17.5 us (10%)
  between operations  13.6 us (8%)
  starting transfers between devices  12.6 us (7%)
  other arithmetic  12 us (7%)
  matrix products  7.72 us (4%)
    psum x3, waiting for transfers between devices, summed_full(): return lax.psum(term.astype(jnp.bfloat16), 'mp').astype(jnp.float32)  86.6 us
    all_gather x1, blocking collectives, per_device(): lax.all_gather(pair_list, 'pairs', axis=0, tiled=True)  13 us
    all_gather x1, blocking collectives, per_device(): start = lax.all_gather(slices, 'mp', axis=2, tiled=True)  8.6 us
    rev x2, local copies, waits for them, and re-layouts, partner(): return jnp.flip(paired, axis=1).reshape(shape)  8.14 us
    all_to_all x1, waiting for transfers between devices, per_device(): lax.all_to_all(back.reshape(owners_n, TOKS, quarter), 'pairs', split_axis...  5.53 us
    all_to_all x1, starting transfers between devices, per_device(): lax.all_to_all(back_weight, 'pairs', split_axis=0, concat_axis=0, tiled=T...  4.6 us
    all_to_all x1, starting transfers between devices, per_device(): lax.all_to_all(back.reshape(owners_n, TOKS, quarter), 'pairs', split_axis...  4.6 us
    reduce_sum x4, other arithmetic, layer_norm(): center = values - jnp.mean(values, axis=-1, keepdims=True)  3.78 us
  transfers between devices with their start and end apart: 6, of which 5 were waited for; matrix products, arithmetic and copies ran while one was open for 3% of the time, Pallas kernels for 0%

commit v1 on v0

--- a/solution.py
+++ b/solution.py
@@ -6,6 +6,12 @@
 HEAD = 64
 TOKS = 32
 EPSILON = 1e-06
+
+
+def add_all(x, name):
+    terms = lax.all_gather(x, name, axis=0, tiled=False)
+    total = terms.sum(axis=0)
+    return total
 
 
 def layer_norm(values, gain):
@@ -35,7 +41,7 @@
 
 
 def summed_full(term):
-    return lax.psum(term.astype(jnp.bfloat16), "mp").astype(jnp.float32)
+    return add_all(term.astype(jnp.bfloat16), "mp").astype(jnp.float32)
 
 
 def per_device(

time: 181 us -> 87.4 us (0.48)
  waiting for transfers between devices: 95.8 us -> 8 us
  blocking collectives: 21.6 us -> 47.7 us
  between operations: 13.6 us -> 0.48 us
  other arithmetic: 12 us -> 3.46 us
  local copies, waits for them, and re-layouts: 17.5 us -> 9.82 us
  matrix products: 7.72 us -> 5.69 us
    psum x3 -> x0, waiting for transfers between devices: 86.6 us -> none  [summed_full(): return lax.psum(term.astype(jnp.bfloat16), 'mp').astype(jnp.float32)]
    all_gather x0 -> x3, blocking collectives: none -> 26.2 us  [add_all(): terms = lax.all_gather(x, name, axis=0, tiled=False)]
    rev x2 -> x1, local copies, waits for them, and re-layouts: 8.14 us -> 0.03 us  [partner(): return jnp.flip(paired, axis=1).reshape(shape)]
    reduce_sum x4, other arithmetic: 3.78 us -> 0.48 us  [layer_norm(): center = values - jnp.mean(values, axis=-1, keepdims=True)]
    reduce_sum x4, other arithmetic: 3.23 us -> 0.77 us  [layer_norm(): spread = jnp.mean(center * center, axis=-1, keepdims=True)]
  transfers between devices with their start and end apart: 6 -> 3, of which waited for: 5 -> 2; matrix products, arithmetic and copies ran while one was open for 3% -> 18% of each run, Pallas kernels for 0% -> 0%
where the time goes in v1:
time: 87.4 us; the launch traced here: 86.8 us
  blocking collectives  47.7 us (55%)
  starting transfers between devices  11.6 us (13%)
  local copies, waits for them, and re-layouts  9.82 us (11%)
  waiting for transfers between devices  8 us (9%)
  matrix products  5.69 us (7%)
  other arithmetic  3.46 us (4%)
    all_gather x3, blocking collectives, add_all(): terms = lax.all_gather(x, name, axis=0, tiled=False)  26.2 us
    all_gather x1, blocking collectives, per_device(): lax.all_gather(pair_list, 'pairs', axis=0, tiled=True)  13 us
    all_gather x1, blocking collectives, per_device(): start = lax.all_gather(slices, 'mp', axis=2, tiled=True)  8.6 us
    all_to_all x1, waiting for transfers between devices, per_device(): lax.all_to_all(back.reshape(owners_n, TOKS, quarter), 'pairs', split_axis...  5.53 us
    all_to_all x1, starting transfers between devices, per_device(): lax.all_to_all(back.reshape(owners_n, TOKS, quarter), 'pairs', split_axis...  5.05 us
    all_to_all x1, starting transfers between devices, per_device(): lax.all_to_all(outgoing, 'pairs', split_axis=0, concat_axis=0, tiled=True)  3.28 us
    all_to_all x1, starting transfers between devices, per_device(): lax.all_to_all(back_weight, 'pairs', split_axis=0, concat_axis=0, tiled=T...  3.22 us
    dot_general x1, matrix products, per_device(): jnp.dot(hidden.astype(jnp.bfloat16), mlp_down, preferred_element_type=jnp...  2.72 us
  transfers between devices with their start and end apart: 3, of which 2 were waited for; matrix products, arithmetic and copies ran while one was open for 18% of the time, Pallas kernels for 0%

profile of v1, /device:TPU:0, one launch (start us, length us, event | category | flops | bytes accessed | tf_op | source)
XLA Modules:
  0.0 86.8 jit_solution(9064554680219542718)
XLA Ops:
  0.0 13.0 %all-gather.3 = s32[4,2,2]{2,1,0:T(2,128)S(1)} all-gather(s32[1,2,2]{2,1,0:T(2,128)} %bitcast.102), channel_id=1, replica_groups=mesh['groups'=2,'pairs'=4,'mp'=4] {'pairs'}, dimensions={0}, use_global_device_ids=true | all-gather | bytes 80 | tf_op jit(solution)/shard_map/all_gather | solution.py:69
  13.2 0.1 reduce_max.36
  13.3 1.3 %gather_fusion = bf16[4,32,192]{2,1,0:T(8,128)(2,1)S(1)} fusion(bf16[2,32,192]{2,1,0:T(8,128)(2,1)} %bitcast.100, s32[1024]{0:T(1024)S(1)} %pad_clamp_fusion.1), kind=kCustom, calls=%fused_computation | custom fusion | bytes 98320 | tf_op jit(solution)/shard_map/jit(_take)/gather | solution.py:73
  14.6 0.7 select_select_fusion
  15.3 3.3 %all-to-all-start = ((bf16[4,32,192]{2,1,0:T(8,128)(2,1)}), bf16[4,32,192]{2,1,0:T(8,128)(2,1)S(1)}, u32[]{:S(2)}, u32[]{:S(2)}) async-start(bf16[4,32,192]{2,1,0:T(8,128)(2,1)} %select_select_fusion), calls=%async_computation | async-start | bytes 131072 | tf_op jit(solution)/shard_map/all_to_all | solution.py:75
  18.6 0.8 reshape.327
  19.4 0.8 reshape.325
  20.2 0.8 mul.147
  21.0 0.1 mul.149
  21.2 0.1 fusion.9
  21.3 0.6 copy.92
  21.9 2.5 %all-to-all-done = bf16[4,32,192]{2,1,0:T(8,128)(2,1)S(1)} async-done(((bf16[4,32,192]{2,1,0:T(8,128)(2,1)}), bf16[4,32,192]{2,1,0:T(8,128)(2,1)S(1)}, u32[]{:S(2)}, u32[]{:S(2)}) %all-to-all-start) | async-done | bytes 49184 | tf_op jit(solution)/shard_map/all_to_all | solution.py:75
  24.3 3.2 %all-to-all-start.2 = ((bf16[4,1,32]{2,1,0:T(2,128)(2,1)}), bf16[4,1,32]{2,1,0:T(2,128)(2,1)S(1)}, u32[]{:S(2)}, u32[]{:S(2)}) async-start(bf16[4,1,32]{2,1,0:T(2,128)(2,1)} %copy.92), calls=%async_computation.2 | async-start | bytes 4096 | tf_op jit(solution)/shard_map/all_to_all | solution.py:119
  27.6 0.6 gather_fusion.1
  28.2 0.2 copy.73
  28.4 8.6 %all_gather.25 = bf16[4,32,768]{1,0,2:T(4,128)(2,1)S(1)} all-gather(bf16[4,32,192]{1,0,2:T(4,128)(2,1)S(1)} %copy.73), channel_id=1, replica_groups=mesh['groups'=2,'pairs'=4,'mp'=4] {'mp'}, dimensions={2}, use_global_device_ids=true | all-gather | bytes 245760 | tf_op jit(solution)/shard_map/all_gather | solution.py:78
  37.0 0.5 copy.74
  37.5 0.1 convert_reduce_fusion
  37.6 0.2 fusion.17
  37.9 0.1 reverse_reduce_fusion
  38.1 0.2 multiply_reduce_fusion.2
  38.4 0.2 fusion.20
  38.7 0.4 fusion.123
  39.1 0.1 reshape.367
  39.2 0.1 reshape.368
  39.4 0.2 convolution_multiply_fusion.1
  39.7 0.1 reshape.366
  39.9 0.3 fusion.6
  40.2 0.1 reshape.329
  40.4 0.2 convolution_convert_fusion.3
  40.6 8.7 %all-gather = bf16[512,768]{1,0:T(8,128)(2,1)S(1)} all-gather(bf16[128,768]{1,0:T(8,128)(2,1)S(1)} %convolution_convert_fusion.3), channel_id=2, replica_groups=mesh['groups'=2,'pairs'=4,'mp'=4] {'mp'}, dimensions={0}, use_global_device_ids=true | all-gather | bytes 983040 | tf_op jit(solution)/shard_map/all_gather | solution.py:12
  49.3 0.1 reduce_sum.129
  49.4 0.1 fusion.74
  49.7 0.2 multiply_reduce_fusion.1
  50.0 0.1 multiply_convert_fusion.1
  50.1 0.3 copy-done.4
  50.4 0.2 convolution_convert_fusion.6
  50.6 0.1 reshape.370
  50.9 0.1 fusion.15
  51.1 0.3 fusion.124
  51.4 0.1 reshape.371
  51.6 0.2 convolution_multiply_fusion
  51.9 0.1 reshape.369
  52.0 0.3 fusion.7
  52.4 0.1 reshape.333
  52.5 0.2 convolution_convert_fusion.2
  52.8 8.7 %all-gather.1 = bf16[512,768]{1,0:T(8,128)(2,1)S(1)} all-gather(bf16[128,768]{1,0:T(8,128)(2,1)S(1)} %convolution_convert_fusion.2), channel_id=3, replica_groups=mesh['groups'=2,'pairs'=4,'mp'=4] {'mp'}, dimensions={0}, use_global_device_ids=true | all-gather | bytes 983040 | tf_op jit(solution)/shard_map/all_gather | solution.py:12
  61.5 0.1 reduce_sum.135
  61.7 0.1 fusion.79
  61.9 0.2 multiply_reduce_fusion
  62.2 0.1 copy-done.9
  62.4 2.7 %convolution_convert_fusion.1 = bf16[128,768]{1,0:T(8,128)(2,1)S(1)} fusion(bf16[768,768]{1,0:T(8,128)(2,1)S(1)} %copy-done, bf16[768,768]{1,0:T(8,128)(2,1)} %param.26, f32[128,768]{1,0:T(8,128)S(1)} %fusion.28, f32[768]{0:T(1024)S(1)} %copy-done.9, f32[128]{0:T(128)S(1)} %rsqrt.51, f32[128]{0:T(128)S(1)} %div.105), kind=kOutput, calls=%fused_computation.7 | convolution fusion | flops 308871168 | bytes 2953216 | tf_op jit(solution)/shard_map/dot_general | solution.py:105
  65.1 8.7 %all-gather.2 = bf16[512,768]{1,0:T(8,128)(2,1)S(1)} all-gather(bf16[128,768]{1,0:T(8,128)(2,1)S(1)} %convolution_convert_fusion.1), channel_id=4, replica_groups=mesh['groups'=2,'pairs'=4,'mp'=4] {'mp'}, dimensions={0}, use_global_device_ids=true | all-gather | bytes 983040 | tf_op jit(solution)/shard_map/all_gather | solution.py:12
  73.8 0.1 reduce_sum.138
  73.9 0.1 dynamic-slice_add_fusion
  74.1 0.1 reshape.334
  74.2 0.2 convolution_convert_fusion
  74.4 0.7 reshape.335
  75.2 5.1 %all-to-all-start.1 = ((bf16[4,32,192]{2,1,0:T(8,128)(2,1)}), bf16[4,32,192]{2,1,0:T(8,128)(2,1)S(1)}, u32[]{:S(2)}, u32[]{:S(2)}) async-start(bf16[4,32,192]{2,1,0:T(8,128)(2,1)} %reshape.335), calls=%async_computation.1 | async-start | bytes 131072 | tf_op jit(solution)/shard_map/all_to_all | solution.py:116
  80.2 0.1 convolution_maximum_fusion
  80.3 0.1 copy.93
  80.4 5.5 %all-to-all-done.1 = bf16[4,32,192]{2,1,0:T(8,128)(2,1)S(1)} async-done(((bf16[4,32,192]{2,1,0:T(8,128)(2,1)}), bf16[4,32,192]{2,1,0:T(8,128)(2,1)S(1)}, u32[]{:S(2)}, u32[]{:S(2)}) %all-to-all-start.1) | async-done | bytes 49184 | tf_op jit(solution)/shard_map/all_to_all | solution.py:116
  86.0 0.2 fusion.8
  86.1 0.6 copy.94
  (57 shorter events, 1.8 us)
Async XLA Ops:
  0.0 62.2 %copy-start = (bf16[768,768]{1,0:T(8,128)(2,1)S(1)}, bf16[768,768]{1,0:T(8,128)(2,1)}, u32[]{:S(2)}) copy-start(bf16[768,768]{1,0:T(8,128)(2,1)} %param.27) | copy-start | bytes 3538948
  15.3 9.0 %all-to-all-start = ((bf16[4,32,192]{2,1,0:T(8,128)(2,1)}), bf16[4,32,192]{2,1,0:T(8,128)(2,1)S(1)}, u32[]{:S(2)}, u32[]{:S(2)}) async-start(bf16[4,32,192]{2,1,0:T(8,128)(2,1)} %select_select_fusion), calls=%async_computation | async-start | bytes 131072 | tf_op jit(solution)/shard_map/all_to_all | solution.py:75
  24.3 50.8 %all-to-all-start.2 = ((bf16[4,1,32]{2,1,0:T(2,128)(2,1)}), bf16[4,1,32]{2,1,0:T(2,128)(2,1)S(1)}, u32[]{:S(2)}, u32[]{:S(2)}) async-start(bf16[4,1,32]{2,1,0:T(2,128)(2,1)} %copy.92), calls=%async_computation.2 | async-start | bytes 4096 | tf_op jit(solution)/shard_map/all_to_all | solution.py:119
  37.0 1.4 %copy-start.6 = (f32[768]{0:T(1024)S(1)}, f32[768]{0:T(1024)}, u32[]{:S(2)}) copy-start(f32[768]{0:T(1024)} %param.17) | copy-start | bytes 9220
  37.5 1.2 %copy-start.1 = (bf16[3,768,192]{1,2,0:T(8,128)(2,1)S(1)}, bf16[3,768,192]{1,2,0:T(8,128)(2,1)}, u32[]{:S(2)}) copy-start(bf16[3,768,192]{1,2,0:T(8,128)(2,1)} %param.21) | copy-start | bytes 2654212
  39.4 1.0 %copy-start.3 = (bf16[192,768]{1,0:T(8,128)(2,1)S(1)}, bf16[192,768]{1,0:T(8,128)(2,1)}, u32[]{:S(2)}) copy-start(bf16[192,768]{1,0:T(8,128)(2,1)} %param.22) | copy-start | bytes 884740
  49.3 0.7 copy-start.7
  49.4 1.0 %copy-start.4 = (bf16[768,192]{0,1:T(8,128)(2,1)S(1)}, bf16[768,192]{0,1:T(8,128)(2,1)}, u32[]{:S(2)}) copy-start(bf16[768,192]{0,1:T(8,128)(2,1)} %param.23) | copy-start | bytes 884740
  49.7 1.2 %copy-start.8 = (f32[768]{0:T(1024)S(1)}, f32[768]{0:T(1024)}, u32[]{:S(2)}) copy-start(f32[768]{0:T(1024)} %param.19) | copy-start | bytes 9220
  50.0 1.1 %copy-start.2 = (bf16[2,768,192]{1,2,0:T(8,128)(2,1)S(1)}, bf16[2,768,192]{1,2,0:T(8,128)(2,1)}, u32[]{:S(2)}) copy-start(bf16[2,768,192]{1,2,0:T(8,128)(2,1)} %param.24) | copy-start | bytes 1769476
  51.6 1.0 %copy-start.5 = (bf16[192,768]{1,0:T(8,128)(2,1)S(1)}, bf16[192,768]{1,0:T(8,128)(2,1)}, u32[]{:S(2)}) copy-start(bf16[192,768]{1,0:T(8,128)(2,1)} %param.25) | copy-start | bytes 884740
  61.7 0.7 copy-start.9
  75.2 10.8 %all-to-all-start.1 = ((bf16[4,32,192]{2,1,0:T(8,128)(2,1)}), bf16[4,32,192]{2,1,0:T(8,128)(2,1)S(1)}, u32[]{:S(2)}, u32[]{:S(2)}) async-start(bf16[4,32,192]{2,1,0:T(8,128)(2,1)} %reshape.335), calls=%async_computation.1 | async-start | bytes 131072 | tf_op jit(solution)/shard_map/all_to_all | solution.py:116
